TPU v7x, 512 devices: a whole 4x4x16 slice. The times are simulated.
512 devices in a mesh: ctx: 32 (over z_hi, y, x), exp: 16 (over z_lo, core).
Axes of the slice: x: 4, y: 4, z: 16 (z_hi: 2, z_lo: 8; z = z_hi * 8 + z_lo), core: 2. Of those that a mesh axis runs over, the one named last changes fastest.
Arguments:
- hidden_in: bfloat16 [4096, 2880], P('ctx'), may hold values from -6 to 6
- query_input: bfloat16 [4096, 2048], P('ctx', 'exp'), may hold values from -16 to 16
- key_heads_input: bfloat16 [4096, 256], P('ctx'), may hold values from -16 to 16
- value_heads_input: bfloat16 [4096, 256], P('ctx'), may hold values from -6 to 6
- sink_logits: float32 [32], P('exp'), may hold values from 0 to 4
- out_proj: bfloat16 [2048, 2880], P('exp'), may hold values from -0.125 to 0.125
- norm_gain: float32 [2880], replicated, may hold values from 0.5 to 1.5
- expert_ids: int32 [4096, 4], P('ctx'), may hold values from 0 to 31, all different within a row; in each aligned block of 128 rows (0 to 127, 128 to 255, ...) at most 20 rows name the same one
- expert_gates: float32 [4096, 4], P('ctx'), may hold values from 0.1 to 1
- gate_up: bfloat16 [32, 2880, 2, 2880], P('ctx', None, None, 'exp'), may hold values from -0.109375 to 0.109375
- down_proj: bfloat16 [32, 2880, 2880], P('ctx', 'exp'), may hold values from -0.109375 to 0.109375
Outputs:
- layer_out: bfloat16 [4096, 2880], P('ctx', 'exp')
Inputs may be any that keep to these rules, and one draw needn't show every extreme that they name: `expert_ids`: each token names 4 different experts; within the 128 tokens of one device no expert is named by more than 20 tokens.
All inputs are finite; a program needn't handle non-finite values.
Results may differ from a plain program's by a relative error of at most 0.02.
Values may be sent and summed in bfloat16 or wider, within the bound.
No kernel may reach another device: no remote copies, remote signals or barrier semaphores. Data moves between devices by JAX's collectives and lax.ppermute only.
A program may use at most 64 MiB of HBM per device.

v0:
```python
import math
import jax
import jax.numpy as jnp
import numpy as np
from jax import lax
from jax.sharding import PartitionSpec as P

D = 2880
QUERY_HEADS = 32
KEY_VALUE_HEADS = 4
HEAD_SIZE = 64
yarn_base = 150000.0
yarn_factor = 32.0
yarn_initial = 4096.0
beta_fast = 32.0
beta_slow = 1.0
neg_large = -1e30


def yarn_frequencies(head_dim):
    half_dim = head_dim // 2

    def correction(rotations):
        return (
            head_dim
            * math.log(yarn_initial / (rotations * 2.0 * math.pi))
            / (2.0 * math.log(yarn_base))
        )

    lower_dim = max(math.floor(correction(beta_fast)), 0)
    upper_dim = min(math.ceil(correction(beta_slow)), head_dim - 1)
    extrap_freq = 1.0 / yarn_base ** (np.arange(0, head_dim, 2) / head_dim)
    interp_freq = extrap_freq / yarn_factor
    ramp_part = np.clip((np.arange(half_dim) - lower_dim) / (upper_dim - lower_dim), 0.0, 1.0)
    extrap_share = 1.0 - ramp_part
    return (interp_freq * (1.0 - extrap_share) + extrap_freq * extrap_share).astype(np.float32)


def rotate_with_yarn(heads_in, token_positions):
    head_dim = heads_in.shape[-1]
    freqs = jnp.asarray(yarn_frequencies(head_dim))
    angles = token_positions.astype(jnp.float32)[:, None] * freqs[None, :]
    factor = 0.1 * math.log(yarn_factor) + 1.0
    cosine = (jnp.cos(angles) * factor)[:, None, :]
    sine = (jnp.sin(angles) * factor)[:, None, :]
    first_half = heads_in[..., : head_dim // 2]
    second_half = heads_in[..., head_dim // 2 :]
    return jnp.concatenate(
        [first_half * cosine - second_half * sine, second_half * cosine + first_half * sine],
        axis=-1,
    )


def route_slots(ids_block, n_experts):
    flat_ids = ids_block.reshape(-1)
    onehot = (flat_ids[:, None] == jnp.arange(n_experts, dtype=jnp.int32)[None, :]).astype(
        jnp.int32
    )
    ranks = jnp.cumsum(onehot, axis=0) - onehot
    return jnp.sum(ranks * onehot, axis=1).reshape(ids_block.shape)


def per_device(
    hidden_in,
    query_input,
    key_heads_input,
    value_heads_input,
    sink_logits,
    out_proj,
    norm_gain,
    expert_ids,
    expert_gates,
    gate_up,
    down_proj,
):
    tok_rows = hidden_in.shape[0]
    ctx_count = lax.axis_size("ctx")
    exp_count = lax.axis_size("exp")
    local_heads = query_input.shape[1] // HEAD_SIZE
    token_positions = lax.axis_index("ctx") * tok_rows + jnp.arange(tok_rows, dtype=jnp.int32)
    q_rot = rotate_with_yarn(
        query_input.astype(jnp.float32).reshape(tok_rows, local_heads, HEAD_SIZE), token_positions
    ).astype(jnp.bfloat16)
    shared_key_head = lax.axis_index("exp") * local_heads // (QUERY_HEADS // KEY_VALUE_HEADS)
    key_block = lax.dynamic_slice_in_dim(key_heads_input, shared_key_head * HEAD_SIZE, HEAD_SIZE, 1)
    value_block = lax.dynamic_slice_in_dim(
        value_heads_input, shared_key_head * HEAD_SIZE, HEAD_SIZE, 1
    )
    key_rot = (
        rotate_with_yarn(
            key_block.astype(jnp.float32).reshape(tok_rows, 1, HEAD_SIZE), token_positions
        )
        .reshape(tok_rows, HEAD_SIZE)
        .astype(jnp.bfloat16)
    )
    key_value = jnp.concatenate([key_rot, value_block], axis=1)
    score_scale = 1.0 / math.sqrt(HEAD_SIZE)
    block_part = lax.all_gather(key_value, "ctx", axis=0, tiled=True)
    run_max = jnp.broadcast_to(sink_logits[:, None], (local_heads, tok_rows))
    run_total = jnp.ones((local_heads, tok_rows), jnp.float32)
    run_sum = jnp.zeros((local_heads, tok_rows, HEAD_SIZE), jnp.float32)
    key_count = block_part.shape[0]
    key_part = block_part[:, :HEAD_SIZE]
    value_part = block_part[:, HEAD_SIZE:].astype(jnp.float32)
    scores = (
        jnp.einsum("rhd,kd->hrk", q_rot, key_part, preferred_element_type=jnp.float32) * score_scale
    )
    key_pos = jnp.arange(key_count, dtype=jnp.int32)
    visible = token_positions[:, None] >= key_pos[None, :]
    scores = jnp.where(visible[None, :, :], scores, neg_large)
    new_max = jnp.maximum(run_max, jnp.max(scores, axis=2))
    weights = jnp.exp(scores - new_max[:, :, None])
    factor = jnp.exp(run_max - new_max)
    run_total = run_total * factor + jnp.sum(weights, axis=2)
    run_sum = run_sum * factor[:, :, None] + jnp.einsum(
        "hrk,kd->hrd", weights, value_part, precision=lax.Precision.HIGHEST
    )
    run_max, run_total, run_sum = (new_max, run_total, run_sum)
    attended = (
        (run_sum / run_total[:, :, None])
        .transpose(1, 0, 2)
        .reshape(tok_rows, local_heads * HEAD_SIZE)
        .astype(jnp.bfloat16)
    )
    head_part = jnp.dot(attended, out_proj, preferred_element_type=jnp.float32)
    residual = hidden_in.astype(jnp.float32) + lax.psum(
        head_part.astype(jnp.bfloat16), "exp"
    ).astype(jnp.float32)
    mean_square = jnp.mean(residual * residual, axis=1, keepdims=True)
    normed = (residual * lax.rsqrt(mean_square + 1e-05) * norm_gain[None, :]).astype(jnp.bfloat16)
    exp_local = gate_up.shape[0]
    n_experts = exp_local * ctx_count
    top_count = expert_ids.shape[1]
    capacity = max(2, tok_rows * top_count * 5 // (4 * n_experts))
    slot_index = route_slots(expert_ids, n_experts)
    dest_row = expert_ids * capacity + slot_index
    spread_rows = jnp.broadcast_to(normed[:, None, :], (tok_rows, top_count, D)).reshape(
        tok_rows * top_count, D
    )
    send_rows = (
        jnp.zeros((n_experts * capacity, D), jnp.bfloat16).at[dest_row.reshape(-1)].set(spread_rows)
    )
    bucket_rows = ctx_count * capacity
    unit_count = gate_up.shape[-1]
    col_width = D // exp_count
    weights_flat = gate_up.reshape(exp_local, D, 2 * unit_count)
    received = lax.all_to_all(
        send_rows.reshape(ctx_count, exp_local * capacity, D),
        "ctx",
        split_axis=0,
        concat_axis=0,
        tiled=True,
    )
    expert_rows = (
        received.reshape(ctx_count, exp_local, capacity, D)
        .transpose(1, 0, 2, 3)
        .reshape(exp_local, bucket_rows, D)
    )
    gate_up_out = jnp.einsum(
        "erd,edf->erf", expert_rows, weights_flat, preferred_element_type=jnp.float32
    )
    gate_up_out = gate_up_out.reshape(exp_local, bucket_rows, 2, unit_count)
    gate_value = gate_up_out[:, :, 0]
    up_value = gate_up_out[:, :, 1]
    activated = ((up_value + 1.0) * gate_value * jax.nn.sigmoid(1.702 * gate_value)).astype(
        jnp.bfloat16
    )
    partial_value = jnp.einsum(
        "erf,efd->erd", activated, down_proj, preferred_element_type=jnp.float32
    )
    partial_rounded = partial_value.astype(jnp.bfloat16)
    outgoing = partial_rounded.reshape(exp_local, ctx_count, capacity, D).transpose(1, 0, 2, 3)
    returned = lax.all_to_all(
        outgoing.reshape(ctx_count, exp_local * capacity, D),
        "ctx",
        split_axis=0,
        concat_axis=0,
        tiled=True,
    )
    picked_rows = returned.reshape(n_experts * capacity, D)[dest_row]
    gated = jnp.sum(expert_gates[:, :, None] * picked_rows.astype(jnp.float32), axis=1)
    moe_cols = lax.psum_scatter(
        gated.astype(jnp.bfloat16), "exp", scatter_dimension=1, tiled=True
    ).astype(jnp.float32)
    residual_cols = lax.dynamic_slice_in_dim(
        residual, lax.axis_index("exp") * col_width, col_width, 1
    )
    return (residual_cols + moe_cols).astype(jnp.bfloat16)


def solution(mesh):
    placed = (
        P("ctx", None),
        P("ctx", "exp"),
        P("ctx", None),
        P("ctx", None),
        P("exp"),
        P("exp", None),
        P(),
        P("ctx", None),
        P("ctx", None),
        P("ctx", None, None, "exp"),
        P("ctx", "exp", None),
    )
    return jax.shard_map(
        per_device, mesh=mesh, in_specs=placed, out_specs=P("ctx", "exp"), check_vma=False
    )
```

profile of v0, /device:TPU:8, one launch (start us, length us, event | category | flops | bytes accessed | tf_op | source)
XLA Modules:
  0.0 880.9 jit_solution(616412392526156827)
XLA Ops:
  6.5 1.0 constant_dynamic-slice_fusion
  7.7 0.8 fusion.35
  8.6 0.6 pad_maximum_fusion
  9.2 0.8 copy.51
  10.1 0.8 copy.54
  11.0 0.8 fusion.41
  11.8 0.3 iota_compare_fusion
  12.2 119.5 %all-gather.2.cloned.1.call-done = bf16[4096,128]{0,1:T(8,128)(2,1)} async-done(((bf16[128,128]{0,1:T(8,128)(2,1)}), bf16[4096,128]{0,1:T(8,128)(2,1)}) %all-gather.2.cloned.1.call-update) | async-done | bytes 1048592 | tf_op jit(solution)/shard_map/all_gather | solution.py:98
  131.7 2.0 fusion.47
  133.8 0.6 fusion.5
  134.4 2.1 fusion.16
  136.5 1.2 convolution_convert_fusion.1
  137.9 1.3 reduce-window.6
  139.2 0.2 slice_reduce_fusion
  139.8 0.1 copy.58
  139.9 0.1 reshape.374
  140.0 186.8 %all-reduce.4.cloned.1.call-done = bf16[128,2880]{0,1:T(8,128)(2,1)} async-done(((bf16[128,2880]{0,1:T(8,128)(2,1)}), bf16[128,2880]{0,1:T(8,128)(2,1)}) %all-reduce.4.cloned.1.call-update) | async-done | bytes 737296 | tf_op jit(solution)/shard_map/psum | solution.py:126
  326.8 1.5 multiply_reduce_fusion.1
  328.3 2.7 multiply_convert_fusion
  331.0 0.4 copy.59
  331.4 2.4 broadcast_in_dim.27
  333.8 5.6 reshape.397
  339.4 8.4 scatter_custom_fusion
  347.7 6.4 reshape.376
  354.1 17.0 %all-to-all-start = ((bf16[32,20,2880]{2,1,0:T(8,128)(2,1)}), bf16[32,20,2880]{2,1,0:T(8,128)(2,1)}, u32[]{:S(2)}, u32[]{:S(2)}) async-start(bf16[32,20,2880]{2,1,0:T(8,128)(2,1)} %reshape.376), calls=%async_computation | async-start | bytes 9043968 | tf_op jit(solution)/shard_map/all_to_all | solution.py:147
  371.1 1.8 copy.60
  372.9 2.3 reshape.378
  375.1 2.1 dot_general.28
  377.2 174.9 %all-to-all-done = bf16[32,20,2880]{2,1,0:T(8,128)(2,1)} async-done(((bf16[32,20,2880]{2,1,0:T(8,128)(2,1)}), bf16[32,20,2880]{2,1,0:T(8,128)(2,1)}, u32[]{:S(2)}, u32[]{:S(2)}) %all-to-all-start) | async-done | bytes 3686432 | tf_op jit(solution)/shard_map/all_to_all | solution.py:147
  552.2 6.6 reshape.377
  558.7 4.0 fusion.10
  562.8 3.3 convolution_convert_fusion
  566.1 6.2 copy.62
  572.3 6.4 reshape_transpose_reshape.4
  578.6 122.0 %all-to-all-start.1 = ((bf16[32,20,2880]{2,1,0:T(8,128)(2,1)}), bf16[32,20,2880]{2,1,0:T(8,128)(2,1)}, u32[]{:S(2)}, u32[]{:S(2)}) async-start(bf16[32,20,2880]{2,1,0:T(8,128)(2,1)} %reshape_transpose_reshape.4), calls=%async_computation.1 | async-start | bytes 9043968 | tf_op jit(solution)/shard_map/all_to_all | solution.py:173
  700.7 0.1 copy.63
  700.9 0.1 copy.53
  701.0 80.2 %all-to-all-done.1 = bf16[32,20,2880]{2,1,0:T(8,128)(2,1)} async-done(((bf16[32,20,2880]{2,1,0:T(8,128)(2,1)}), bf16[32,20,2880]{2,1,0:T(8,128)(2,1)}, u32[]{:S(2)}, u32[]{:S(2)}) %all-to-all-start.1) | async-done | bytes 3686432 | tf_op jit(solution)/shard_map/all_to_all | solution.py:173
  781.2 6.6 reshape.380
  787.8 9.3 %gather_fusion = bf16[512,2880]{1,0:T(8,128)(2,1)} fusion(bf16[640,2880]{1,0:T(8,128)(2,1)} %reshape.380, s32[1024]{0:T(1024)S(1)} %pad_clamp_fusion), kind=kCustom, calls=%fused_computation | custom fusion | bytes 5900288 | tf_op jit(solution)/shard_map/gather | solution.py:180
  797.1 6.6 reshape.403
  803.7 7.1 multiply_reduce_fusion
  810.8 0.4 copy.64
  811.2 57.7 %fusion = bf16[128,192]{0,1:T(8,128)(2,1)S(1)} fusion(bf16[128,2880]{0,1:T(8,128)(2,1)S(1)} %copy.64), kind=kCustom, calls=%all-reduce-scatter | all-reduce-scatter fusion | flops 393217 | bytes 788480
  868.9 1.3 collective-permute-start
  870.2 1.3 dynamic-slice.4
  872.2 0.4 concatenate.14
  872.5 1.5 add_convert_fusion
  (46 shorter events, 1.2 us)
Async XLA Ops:
  6.5 556.2 %copy-start = (bf16[1,180,2880]{2,1,0:T(8,128)(2,1)S(1)}, bf16[1,180,2880]{2,1,0:T(8,128)(2,1)}, u32[]{:S(2)}) copy-start(bf16[1,180,2880]{2,1,0:T(8,128)(2,1)} %param.23) | copy-start | bytes 3110404
  6.5 125.1 %all-gather.2.cloned.1.call-start = ((), (), s32[]{:S(2)}) async-start(), calls=%async_computation.2 | async-start | bytes 1081344 | tf_op jit(solution)/shard_map/all_gather | solution.py:98
  7.6 126.1 %copy-start.8 = (f32[2]{0:T(128)S(1)}, f32[2]{0:T(128)}, u32[]{:S(2)}) copy-start(f32[2]{0:T(128)} %param.17) | copy-start | bytes 28
  9.2 317.6 %all-reduce.4.cloned.1.call-start = ((), (), s32[]{:S(2)}) async-start(), calls=%async_computation.3 | async-start | bytes 1474560 | tf_op jit(solution)/shard_map/psum | solution.py:126
  131.7 2.7 copy-start.4
  133.8 2.7 copy-start.3
  134.4 5.4 copy-start.6
  134.4 192.4 %copy-start.2 = (bf16[128,2880]{0,1:T(8,128)(2,1)S(1)}, bf16[128,2880]{0,1:T(8,128)(2,1)}, u32[]{:S(2)}) copy-start(bf16[128,2880]{0,1:T(8,128)(2,1)} %param.13) | copy-start | bytes 2211844
  134.4 193.9 %copy-start.5 = (f32[2880]{0:T(1024)S(1)}, f32[2880]{0:T(1024)}, u32[]{:S(2)}) copy-start(f32[2880]{0:T(1024)} %param.19) | copy-start | bytes 34564
  354.1 198.1 %all-to-all-start = ((bf16[32,20,2880]{2,1,0:T(8,128)(2,1)}), bf16[32,20,2880]{2,1,0:T(8,128)(2,1)}, u32[]{:S(2)}, u32[]{:S(2)}) async-start(bf16[32,20,2880]{2,1,0:T(8,128)(2,1)} %reshape.376), calls=%async_computation | async-start | bytes 9043968 | tf_op jit(solution)/shard_map/all_to_all | solution.py:147
  578.6 122.2 %copy-start.7 = (f32[128,4]{0,1:T(4,128)S(1)}, f32[128,4]{0,1:T(4,128)}, u32[]{:S(2)}) copy-start(f32[128,4]{0,1:T(4,128)} %param.21) | copy-start | bytes 6148
  578.6 202.6 %all-to-all-start.1 = ((bf16[32,20,2880]{2,1,0:T(8,128)(2,1)}), bf16[32,20,2880]{2,1,0:T(8,128)(2,1)}, u32[]{:S(2)}, u32[]{:S(2)}) async-start(bf16[32,20,2880]{2,1,0:T(8,128)(2,1)} %reshape_transpose_reshape.4), calls=%async_computation.1 | async-start | bytes 9043968 | tf_op jit(solution)/shard_map/all_to_all | solution.py:173
  797.1 77.0 %copy-start.1 = (bf16[1,180,2880]{2,1,0:T(8,128)(2,1)S(1)}, bf16[1,180,2880]{2,1,0:T(8,128)(2,1)}, u32[]{:S(2)}) copy-start(bf16[1,180,2880]{2,1,0:T(8,128)(2,1)} %param.23) | copy-start | bytes 3110404
  868.9 3.2 collective-permute-start
Sparse Core Ops, SparseCore 0:
  11.4 120.1 all-gather.1
  137.8 188.8 all-reduce.3
where the time goes:
time: 883 us; the launch traced here: 881 us
  waiting for transfers between devices  561 us (64%)
  starting transfers between devices  140 us (16%)
  local copies, waits for them, and re-layouts  76.8 us (9%)
  blocking collectives  57.7 us (7%)
  other arithmetic  17.7 us (2%)
  between operations  14.3 us (2%)
  matrix products  12.6 us (1%)
    psum x1, waiting for transfers between devices, per_device(): lax.psum(head_part.astype(jnp.bfloat16), 'exp').astype(jnp.float32)  187 us
    all_to_all x1, waiting for transfers between devices, per_device(): lax.all_to_all(send_rows.reshape(ctx_count, exp_local * capacity, D), 'ct...  175 us
    all_to_all x1, starting transfers between devices, per_device(): lax.all_to_all(outgoing.reshape(ctx_count, exp_local * capacity, D), 'ctx...  122 us
    all_gather x1, waiting for transfers between devices, per_device(): block_part = lax.all_gather(key_value, 'ctx', axis=0, tiled=True)  119 us
    all_to_all x1, waiting for transfers between devices, per_device(): lax.all_to_all(outgoing.reshape(ctx_count, exp_local * capacity, D), 'ctx...  80.2 us
    unnamed x1, blocking collectives  57.7 us
  transfers between devices with their start and end apart: 5, of which 4 were waited for; matrix products, arithmetic and copies ran while one was open for 1% of the time, Pallas kernels for 0%

commit v1 on v0

--- a/solution.py
+++ b/solution.py
@@ -95,7 +95,9 @@
     )
     key_value = jnp.concatenate([key_rot, value_block], axis=1)
     score_scale = 1.0 / math.sqrt(HEAD_SIZE)
-    block_part = lax.all_gather(key_value, "ctx", axis=0, tiled=True)
+    block_part = jnp.concatenate(
+        lax.all_to_all(jnp.stack([key_value] * lax.axis_size("ctx")), "ctx", 0, 0), axis=0
+    )
     run_max = jnp.broadcast_to(sink_logits[:, None], (local_heads, tok_rows))
     run_total = jnp.ones((local_heads, tok_rows), jnp.float32)
     run_sum = jnp.zeros((local_heads, tok_rows, HEAD_SIZE), jnp.float32)

time: 883 us -> 839 us (0.950)
  waiting for transfers between devices: 561 us -> 500 us
  starting transfers between devices: 140 us -> 161 us
    all_gather x1 -> x0, waiting for transfers between devices: 119 us -> none  [per_device(): block_part = lax.all_gather(key_value, 'ctx', axis=0, tiled=True)]
    psum x1, waiting for transfers between devices: 187 us -> 217 us  [per_device(): lax.psum(head_part.astype(jnp.bfloat16), 'exp').astype(jnp.float32)]
    all_to_all x0 -> x1, waiting for transfers between devices: none -> 27.8 us  [per_device(): lax.all_to_all(jnp.stack([key_value] * lax.axis_size('ctx')), 'ctx', 0, 0)]
    all_to_all x0 -> x1, starting transfers between devices: none -> 20.8 us  [per_device(): lax.all_to_all(jnp.stack([key_value] * lax.axis_size('ctx')), 'ctx', 0, 0)]
where the time goes in v1:
time: 839 us; the launch traced here: 838 us
  waiting for transfers between devices  500 us (60%)
  starting transfers between devices  161 us (19%)
  local copies, waits for them, and re-layouts  76.8 us (9%)
  blocking collectives  57.7 us (7%)
  other arithmetic  16.4 us (2%)
  between operations  14.4 us (2%)
  matrix products  11.5 us (1%)
    psum x1, waiting for transfers between devices, per_device(): lax.psum(head_part.astype(jnp.bfloat16), 'exp').astype(jnp.float32)  217 us
    all_to_all x1, waiting for transfers between devices, per_device(): lax.all_to_all(send_rows.reshape(ctx_count, exp_local * capacity, D), 'ct...  175 us
    all_to_all x1, starting transfers between devices, per_device(): lax.all_to_all(outgoing.reshape(ctx_count, exp_local * capacity, D), 'ctx...  122 us
    all_to_all x1, waiting for transfers between devices, per_device(): lax.all_to_all(outgoing.reshape(ctx_count, exp_local * capacity, D), 'ctx...  80.3 us
    unnamed x1, blocking collectives  57.7 us
    all_to_all x1, waiting for transfers between devices, per_device(): lax.all_to_all(jnp.stack([key_value] * lax.axis_size('ctx')), 'ctx', 0, 0)  27.8 us
    all_to_all x1, starting transfers between devices, per_device(): lax.all_to_all(jnp.stack([key_value] * lax.axis_size('ctx')), 'ctx', 0, 0)  20.8 us
    all_to_all x1, starting transfers between devices, per_device(): lax.all_to_all(send_rows.reshape(ctx_count, exp_local * capacity, D), 'ct...  17 us
  transfers between devices with their start and end apart: 5, of which 4 were waited for; matrix products, arithmetic and copies ran while one was open for 1% of the time, Pallas kernels for 0%

profile of v1, /device:TPU:8, one launch (start us, length us, event | category | flops | bytes accessed | tf_op | source)
XLA Modules:
  0.0 837.6 jit_solution(12530415360333547262)
XLA Ops:
  6.5 1.0 constant_dynamic-slice_fusion
  7.7 0.8 fusion.35
  8.6 1.2 stack.2
  9.8 20.8 %all-to-all-start = ((bf16[32,128,128]{1,2,0:T(8,128)(2,1)}), bf16[32,128,128]{1,2,0:T(8,128)(2,1)S(1)}, u32[]{:S(2)}, u32[]{:S(2)}) async-start(bf16[32,128,128]{1,2,0:T(8,128)(2,1)} %stack.2), calls=%async_computation | async-start | bytes 2097152 | tf_op jit(solution)/shard_map/all_to_all | solution.py:99
  30.8 0.1 copy.53
  31.0 0.1 fusion.41
  31.2 0.3 iota_compare_fusion
  31.5 27.8 %all-to-all-done = bf16[32,128,128]{1,2,0:T(8,128)(2,1)S(1)} async-done(((bf16[32,128,128]{1,2,0:T(8,128)(2,1)}), bf16[32,128,128]{1,2,0:T(8,128)(2,1)S(1)}, u32[]{:S(2)}, u32[]{:S(2)}) %all-to-all-start) | async-done | bytes 1048608 | tf_op jit(solution)/shard_map/all_to_all | solution.py:99
  59.4 0.1 copy_bitcast_fusion
  59.5 0.9 fusion.47
  60.5 0.6 fusion.5
  61.1 2.1 fusion.16
  63.2 1.2 convolution_convert_fusion.1
  64.6 1.3 reduce-window.6
  65.9 0.2 slice_reduce_fusion
  66.5 0.1 copy.57
  66.7 216.7 %all-reduce.4.cloned.1.call-done = bf16[128,2880]{0,1:T(8,128)(2,1)} async-done(((bf16[128,2880]{0,1:T(8,128)(2,1)}), bf16[128,2880]{0,1:T(8,128)(2,1)}) %all-reduce.4.cloned.1.call-update) | async-done | bytes 737296 | tf_op jit(solution)/shard_map/psum | solution.py:128
  283.5 1.5 multiply_reduce_fusion.1
  285.0 2.7 multiply_convert_fusion
  287.7 0.4 copy.58
  288.1 2.4 broadcast_in_dim.27
  290.5 5.6 reshape.403
  296.1 8.4 scatter_custom_fusion
  304.4 6.4 reshape.382
  310.8 17.0 %all-to-all-start.1 = ((bf16[32,20,2880]{2,1,0:T(8,128)(2,1)}), bf16[32,20,2880]{2,1,0:T(8,128)(2,1)}, u32[]{:S(2)}, u32[]{:S(2)}) async-start(bf16[32,20,2880]{2,1,0:T(8,128)(2,1)} %reshape.382), calls=%async_computation.1 | async-start | bytes 9043968 | tf_op jit(solution)/shard_map/all_to_all | solution.py:149
  327.8 1.8 copy.59
  329.6 2.3 reshape.384
  331.8 2.1 dot_general.28
  333.9 174.9 %all-to-all-done.1 = bf16[32,20,2880]{2,1,0:T(8,128)(2,1)} async-done(((bf16[32,20,2880]{2,1,0:T(8,128)(2,1)}), bf16[32,20,2880]{2,1,0:T(8,128)(2,1)}, u32[]{:S(2)}, u32[]{:S(2)}) %all-to-all-start.1) | async-done | bytes 3686432 | tf_op jit(solution)/shard_map/all_to_all | solution.py:149
  508.9 6.6 reshape.383
  515.4 4.0 fusion.10
  519.5 3.3 convolution_convert_fusion
  522.8 6.2 copy.61
  529.0 6.4 reshape_transpose_reshape.4
  535.3 122.0 %all-to-all-start.2 = ((bf16[32,20,2880]{2,1,0:T(8,128)(2,1)}), bf16[32,20,2880]{2,1,0:T(8,128)(2,1)}, u32[]{:S(2)}, u32[]{:S(2)}) async-start(bf16[32,20,2880]{2,1,0:T(8,128)(2,1)} %reshape_transpose_reshape.4), calls=%async_computation.2 | async-start | bytes 9043968 | tf_op jit(solution)/shard_map/all_to_all | solution.py:175
  657.3 0.1 copy.62
  657.6 0.1 copy.52
  657.7 80.3 %all-to-all-done.2 = bf16[32,20,2880]{2,1,0:T(8,128)(2,1)} async-done(((bf16[32,20,2880]{2,1,0:T(8,128)(2,1)}), bf16[32,20,2880]{2,1,0:T(8,128)(2,1)}, u32[]{:S(2)}, u32[]{:S(2)}) %all-to-all-start.2) | async-done | bytes 3686432 | tf_op jit(solution)/shard_map/all_to_all | solution.py:175
  738.0 6.6 reshape.386
  744.5 9.3 %gather_fusion = bf16[512,2880]{1,0:T(8,128)(2,1)} fusion(bf16[640,2880]{1,0:T(8,128)(2,1)} %reshape.386, s32[1024]{0:T(1024)S(1)} %pad_clamp_fusion), kind=kCustom, calls=%fused_computation | custom fusion | bytes 5900288 | tf_op jit(solution)/shard_map/gather | solution.py:182
  753.8 6.6 reshape.409
  760.4 7.1 multiply_reduce_fusion
  767.5 0.4 copy.63
  767.9 57.7 %fusion = bf16[128,192]{0,1:T(8,128)(2,1)S(1)} fusion(bf16[128,2880]{0,1:T(8,128)(2,1)S(1)} %copy.63), kind=kCustom, calls=%all-reduce-scatter | all-reduce-scatter fusion | flops 393217 | bytes 788480
  825.6 1.3 collective-permute-start
  826.9 1.3 dynamic-slice.4
  828.8 0.4 concatenate.14
  829.2 1.5 add_convert_fusion
  (49 shorter events, 1.4 us)
Async XLA Ops:
  6.5 512.9 %copy-start = (bf16[1,180,2880]{2,1,0:T(8,128)(2,1)S(1)}, bf16[1,180,2880]{2,1,0:T(8,128)(2,1)}, u32[]{:S(2)}) copy-start(bf16[1,180,2880]{2,1,0:T(8,128)(2,1)} %param.23) | copy-start | bytes 3110404
  6.5 24.5 %copy-start.7 = (f32[32]{0:T(128)S(1)}, f32[32]{0:T(128)}, u32[]{:S(2)}) copy-start(f32[32]{0:T(128)} %constant.73.clone) | copy-start | bytes 388
  6.5 24.1 %copy-start.4 = (bf16[128,128]{1,0:T(8,128)(2,1)S(1)}, bf16[128,128]{1,0:T(8,128)(2,1)}, u32[]{:S(2)}) copy-start(bf16[128,128]{1,0:T(8,128)(2,1)} %param.14) | copy-start | bytes 98308
  6.5 24.2 %copy-start.6 = (s32[128,4]{0,1:T(4,128)S(1)}, s32[128,4]{0,1:T(4,128)}, u32[]{:S(2)}) copy-start(s32[128,4]{0,1:T(4,128)} %param.20) | copy-start | bytes 6148
  9.8 49.6 %all-to-all-start = ((bf16[32,128,128]{1,2,0:T(8,128)(2,1)}), bf16[32,128,128]{1,2,0:T(8,128)(2,1)S(1)}, u32[]{:S(2)}, u32[]{:S(2)}) async-start(bf16[32,128,128]{1,2,0:T(8,128)(2,1)} %stack.2), calls=%async_computation | async-start | bytes 2097152 | tf_op jit(solution)/shard_map/all_to_all | solution.py:99
  30.6 252.9 %all-reduce.4.cloned.1.call-start = ((), (), s32[]{:S(2)}) async-start(), calls=%async_computation.3 | async-start | bytes 1474560 | tf_op jit(solution)/shard_map/psum | solution.py:128
  31.5 28.9 %copy-start.9 = (f32[2]{0:T(128)S(1)}, f32[2]{0:T(128)}, u32[]{:S(2)}) copy-start(f32[2]{0:T(128)} %param.17) | copy-start | bytes 28
  60.5 2.7 copy-start.3
  61.1 222.4 %copy-start.2 = (bf16[128,2880]{0,1:T(8,128)(2,1)S(1)}, bf16[128,2880]{0,1:T(8,128)(2,1)}, u32[]{:S(2)}) copy-start(bf16[128,2880]{0,1:T(8,128)(2,1)} %param.13) | copy-start | bytes 2211844
  61.1 223.9 %copy-start.5 = (f32[2880]{0:T(1024)S(1)}, f32[2880]{0:T(1024)}, u32[]{:S(2)}) copy-start(f32[2880]{0:T(1024)} %param.19) | copy-start | bytes 34564
  310.8 198.1 %all-to-all-start.1 = ((bf16[32,20,2880]{2,1,0:T(8,128)(2,1)}), bf16[32,20,2880]{2,1,0:T(8,128)(2,1)}, u32[]{:S(2)}, u32[]{:S(2)}) async-start(bf16[32,20,2880]{2,1,0:T(8,128)(2,1)} %reshape.382), calls=%async_computation.1 | async-start | bytes 9043968 | tf_op jit(solution)/shard_map/all_to_all | solution.py:149
  535.3 122.2 %copy-start.8 = (f32[128,4]{0,1:T(4,128)S(1)}, f32[128,4]{0,1:T(4,128)}, u32[]{:S(2)}) copy-start(f32[128,4]{0,1:T(4,128)} %param.21) | copy-start | bytes 6148
  535.3 202.6 %all-to-all-start.2 = ((bf16[32,20,2880]{2,1,0:T(8,128)(2,1)}), bf16[32,20,2880]{2,1,0:T(8,128)(2,1)}, u32[]{:S(2)}, u32[]{:S(2)}) async-start(bf16[32,20,2880]{2,1,0:T(8,128)(2,1)} %reshape_transpose_reshape.4), calls=%async_computation.2 | async-start | bytes 9043968 | tf_op jit(solution)/shard_map/all_to_all | solution.py:175
  753.8 76.9 %copy-start.1 = (bf16[1,180,2880]{2,1,0:T(8,128)(2,1)S(1)}, bf16[1,180,2880]{2,1,0:T(8,128)(2,1)}, u32[]{:S(2)}) copy-start(bf16[1,180,2880]{2,1,0:T(8,128)(2,1)} %param.23) | copy-start | bytes 3110404
  825.6 3.2 collective-permute-start
Sparse Core Ops, SparseCore 0:
  64.6 218.8 all-reduce.3
